TPU v7x, 512 devices: a whole 4x4x16 slice. The times are simulated.
512 devices in a mesh: blk: 16 (over x_hi, y, core), wide: 32 (over x_lo, z).
Axes of the slice: x: 4 (x_hi: 2, x_lo: 2; x = x_hi * 2 + x_lo), y: 4, z: 16, core: 2. Of those that a mesh axis runs over, the one named last changes fastest.
Arguments:
- series: bfloat16 [90112, 640], P(('blk', 'wide'))
- scrub_mask: int32 [640], replicated, may hold values from 0 to 1, as said below
- seed_index: int32 [4096], P(('blk', 'wide')), may hold values from 0 to 90111, as said below
Outputs:
- dispersion: bfloat16 [16, 5632, 4096], P(None, 'wide', 'blk')
- statistic: bfloat16 [16, 5632, 4096], P(None, 'wide', 'blk')
Inputs may be any that keep to these rules, and one draw needn't show every extreme that they name: Entry i of seed_index lies among the rows (i // 8) * 176 to (i // 8 + 1) * 176 - 1, and the 8 entries of one such block are distinct. `scrub_mask`: every frame of even position is kept.
All inputs are finite; a program needn't handle non-finite values.
Results may differ from a plain program's by a relative error of at most 0.0057.
Values may be sent and summed in bfloat16 or wider, within the bound.
No kernel may reach another device: no remote copies, remote signals or barrier semaphores. Data moves between devices by JAX's collectives and lax.ppermute only.
A program may use at most 128 MiB of HBM per device.

v0:
```python
import jax
import jax.numpy as jnp
from jax import lax
from jax.sharding import PartitionSpec as P

WIN = 60
STRIDE = 30
NWIN = 20
EPSILON = 1e-05
CLIP_LEVEL = 0.99


def shifted(block, axis, distance):
    devices = range(lax.axis_size(axis))
    route = [((i - distance) % len(devices), i) for i in devices]
    return lax.ppermute(block, axis, route)


def fisher_of(values):
    clipped = jnp.clip(values, -CLIP_LEVEL, CLIP_LEVEL)
    return 0.5 * (jnp.log(1.0 + clipped) - jnp.log(1.0 - clipped))


def prepare(raw_rows, scrub_mask):
    values = raw_rows.astype(jnp.float32)
    row_count = values.shape[0]
    weight = scrub_mask.astype(jnp.float32)
    covered = STRIDE * (NWIN + 1)
    pieces = values[:, :covered].reshape(row_count, NWIN + 1, STRIDE)
    framed = jnp.concatenate([pieces[:, :-1], pieces[:, 1:]], axis=2)
    mask_pieces = weight[:covered].reshape(NWIN + 1, STRIDE)
    mask_framed = jnp.concatenate([mask_pieces[:-1], mask_pieces[1:]], axis=1)
    valid_count = jnp.sum(mask_framed, axis=1)
    centre = jnp.sum(framed * mask_framed, axis=2) / valid_count
    centred = (framed - centre[:, :, None]) * mask_framed
    spread = jnp.sum(centred * centred, axis=2)
    windows = (centred * lax.rsqrt(spread + EPSILON)[:, :, None]).astype(jnp.bfloat16)
    total_valid = jnp.sum(weight)
    mean_all = jnp.sum(values * weight, axis=1) / total_valid
    centred_all = (values - mean_all[:, None]) * weight
    spread_all = jnp.sum(centred_all * centred_all, axis=1)
    whole_std = (centred_all * lax.rsqrt(spread_all + EPSILON)[:, None]).astype(jnp.bfloat16)
    return (windows, whole_std)


def compare(target_windows, target_whole, seed_window, seed_whole, total_valid):
    window_corr = jnp.einsum(
        "tnw,snw->nts", target_windows, seed_window, preferred_element_type=jnp.float32
    )
    fisher = fisher_of(window_corr)
    first_moment = jnp.mean(fisher, axis=0)
    second = jnp.mean(fisher * fisher, axis=0)
    dispersion = ((WIN - 3) * (second - first_moment * first_moment)).astype(jnp.bfloat16)
    static = jnp.einsum("tf,sf->ts", target_whole, seed_whole, preferred_element_type=jnp.float32)
    statistic = (jnp.sqrt(total_valid - 3.0) * fisher_of(static)).astype(jnp.bfloat16)
    return (dispersion, statistic)


def body(series, scrub_mask, seed_index):
    row_count = series.shape[0]
    local_rows = seed_index % row_count
    own_seeds = jnp.take(series, local_rows, axis=0)
    total_valid = jnp.sum(scrub_mask.astype(jnp.float32))
    target_windows, target_whole = prepare(series, scrub_mask)
    blocks = lax.axis_size("blk")
    panel_rows = lax.all_gather(own_seeds, "wide", axis=0, tiled=True)
    seed_window, seed_whole = prepare(panel_rows, scrub_mask)
    panel_size = panel_rows.shape[0]
    own_block = lax.axis_index("blk")

    def record(results, source, raw_rows):
        block_windows, block_whole = prepare(raw_rows, scrub_mask)
        dispersion, statistic = compare(
            block_windows, block_whole, seed_window, seed_whole, total_valid
        )
        return (
            lax.dynamic_update_index_in_dim(results[0], dispersion, source, 0),
            lax.dynamic_update_index_in_dim(results[1], statistic, source, 0),
        )

    empty = jnp.zeros((blocks, row_count, panel_size), jnp.bfloat16)
    own_dispersion, own_statistic = compare(
        target_windows, target_whole, seed_window, seed_whole, total_valid
    )
    results = (
        lax.dynamic_update_index_in_dim(empty, own_dispersion, own_block, 0),
        lax.dynamic_update_index_in_dim(empty, own_statistic, own_block, 0),
    )

    def advance(offset, carry):
        stored, moving = carry
        moving = shifted(moving, "blk", 1)
        stored = record(stored, (own_block - offset) % blocks, moving)
        return (stored, moving)

    results, moving = lax.fori_loop(1, blocks, advance, (results, series))
    return (results[0], results[1])


def solution(mesh):
    in_specs = (P(("blk", "wide"), None), P(), P(("blk", "wide")))
    out_specs = (P(None, "wide", "blk"), P(None, "wide", "blk"))
    return jax.shard_map(body, mesh=mesh, in_specs=in_specs, out_specs=out_specs, check_vma=False)
```

profile of v0, /device:TPU:4, one launch (start us, length us, event | category | flops | bytes accessed | tf_op | source)
XLA Modules:
  0.0 359.1 jit_solution(2068689304347063946)
XLA Ops:
  8.9 70.2 %all_gather.3 = bf16[256,640]{1,0:T(8,128)(2,1)S(1)} all-gather(bf16[8,640]{1,0:T(8,128)(2,1)S(1)} %broadcast_select_fusion), channel_id=1, replica_groups=mesh['blk'=16,'wide'=32] {'wide'}, dimensions={0}, use_global_device_ids=true | all-gather | bytes 337920 | tf_op jit(solution)/shard_map/all_gather | solution.py:66
  85.3 2.3 multiply_reduce_fusion.5
  90.4 267.5 %while.20 = (s32[]{:T(128)}, bf16[16,176,256]{2,1,0:T(8,128)(2,1)}, bf16[16,176,256]{2,1,0:T(8,128)(2,1)S(1)}, bf16[176,640]{0,1:T(8,128)(2,1)S(1)}, f32[20,60]{...) while((s32[]{:T(128)}, bf16[16,176,256]{2,1,0:T(8,128)(2,1)}, ...), condition=%wide.region_20.21_spmd, body=%wide.region_13.20_spmd.sunk | while | flops 177675536 | bytes 12591712 | solution.py:96
  92.4 10.0 %collective-permute-done = bf16[176,640]{0,1:T(8,128)(2,1)S(1)} collective-permute-done((bf16[176,640]{0,1:T(8,128)(2,1)S(1)}, bf16[176,640]{0,1:T(8,128)(2,1)S(1)}, u32[]{:S(2)}, u32[]{:S(2)}) %collective-permute-start) | collective-permute-done | bytes 225312 | tf_op jit(solution)/shard_map/while/body/eval_jaxpr/ppermute | solution.py:16
  110.2 10.0 %collective-permute-done = bf16[176,640]{0,1:T(8,128)(2,1)S(1)} collective-permute-done((bf16[176,640]{0,1:T(8,128)(2,1)S(1)}, bf16[176,640]{0,1:T(8,128)(2,1)S(1)}, u32[]{:S(2)}, u32[]{:S(2)}) %collective-permute-start) | collective-permute-done | bytes 225312 | tf_op jit(solution)/shard_map/while/body/eval_jaxpr/ppermute | solution.py:16
  122.6 2.3 multiply_reduce_fusion.21
  128.1 10.0 %collective-permute-done = bf16[176,640]{0,1:T(8,128)(2,1)S(1)} collective-permute-done((bf16[176,640]{0,1:T(8,128)(2,1)S(1)}, bf16[176,640]{0,1:T(8,128)(2,1)S(1)}, u32[]{:S(2)}, u32[]{:S(2)}) %collective-permute-start) | collective-permute-done | bytes 225312 | tf_op jit(solution)/shard_map/while/body/eval_jaxpr/ppermute | solution.py:16
  140.4 2.3 multiply_reduce_fusion.21
  145.9 10.0 %collective-permute-done = bf16[176,640]{0,1:T(8,128)(2,1)S(1)} collective-permute-done((bf16[176,640]{0,1:T(8,128)(2,1)S(1)}, bf16[176,640]{0,1:T(8,128)(2,1)S(1)}, u32[]{:S(2)}, u32[]{:S(2)}) %collective-permute-start) | collective-permute-done | bytes 225312 | tf_op jit(solution)/shard_map/while/body/eval_jaxpr/ppermute | solution.py:16
  158.2 2.3 multiply_reduce_fusion.21
  163.7 10.0 %collective-permute-done = bf16[176,640]{0,1:T(8,128)(2,1)S(1)} collective-permute-done((bf16[176,640]{0,1:T(8,128)(2,1)S(1)}, bf16[176,640]{0,1:T(8,128)(2,1)S(1)}, u32[]{:S(2)}, u32[]{:S(2)}) %collective-permute-start) | collective-permute-done | bytes 225312 | tf_op jit(solution)/shard_map/while/body/eval_jaxpr/ppermute | solution.py:16
  176.1 2.3 multiply_reduce_fusion.21
  181.6 10.0 %collective-permute-done = bf16[176,640]{0,1:T(8,128)(2,1)S(1)} collective-permute-done((bf16[176,640]{0,1:T(8,128)(2,1)S(1)}, bf16[176,640]{0,1:T(8,128)(2,1)S(1)}, u32[]{:S(2)}, u32[]{:S(2)}) %collective-permute-start) | collective-permute-done | bytes 225312 | tf_op jit(solution)/shard_map/while/body/eval_jaxpr/ppermute | solution.py:16
  193.9 2.3 multiply_reduce_fusion.21
  199.4 10.0 %collective-permute-done = bf16[176,640]{0,1:T(8,128)(2,1)S(1)} collective-permute-done((bf16[176,640]{0,1:T(8,128)(2,1)S(1)}, bf16[176,640]{0,1:T(8,128)(2,1)S(1)}, u32[]{:S(2)}, u32[]{:S(2)}) %collective-permute-start) | collective-permute-done | bytes 225312 | tf_op jit(solution)/shard_map/while/body/eval_jaxpr/ppermute | solution.py:16
  211.8 2.3 multiply_reduce_fusion.21
  217.2 10.0 %collective-permute-done = bf16[176,640]{0,1:T(8,128)(2,1)S(1)} collective-permute-done((bf16[176,640]{0,1:T(8,128)(2,1)S(1)}, bf16[176,640]{0,1:T(8,128)(2,1)S(1)}, u32[]{:S(2)}, u32[]{:S(2)}) %collective-permute-start) | collective-permute-done | bytes 225312 | tf_op jit(solution)/shard_map/while/body/eval_jaxpr/ppermute | solution.py:16
  235.1 10.0 %collective-permute-done = bf16[176,640]{0,1:T(8,128)(2,1)S(1)} collective-permute-done((bf16[176,640]{0,1:T(8,128)(2,1)S(1)}, bf16[176,640]{0,1:T(8,128)(2,1)S(1)}, u32[]{:S(2)}, u32[]{:S(2)}) %collective-permute-start) | collective-permute-done | bytes 225312 | tf_op jit(solution)/shard_map/while/body/eval_jaxpr/ppermute | solution.py:16
  252.9 10.0 %collective-permute-done = bf16[176,640]{0,1:T(8,128)(2,1)S(1)} collective-permute-done((bf16[176,640]{0,1:T(8,128)(2,1)S(1)}, bf16[176,640]{0,1:T(8,128)(2,1)S(1)}, u32[]{:S(2)}, u32[]{:S(2)}) %collective-permute-start) | collective-permute-done | bytes 225312 | tf_op jit(solution)/shard_map/while/body/eval_jaxpr/ppermute | solution.py:16
  270.7 10.0 %collective-permute-done = bf16[176,640]{0,1:T(8,128)(2,1)S(1)} collective-permute-done((bf16[176,640]{0,1:T(8,128)(2,1)S(1)}, bf16[176,640]{0,1:T(8,128)(2,1)S(1)}, u32[]{:S(2)}, u32[]{:S(2)}) %collective-permute-start) | collective-permute-done | bytes 225312 | tf_op jit(solution)/shard_map/while/body/eval_jaxpr/ppermute | solution.py:16
  288.6 10.0 %collective-permute-done = bf16[176,640]{0,1:T(8,128)(2,1)S(1)} collective-permute-done((bf16[176,640]{0,1:T(8,128)(2,1)S(1)}, bf16[176,640]{0,1:T(8,128)(2,1)S(1)}, u32[]{:S(2)}, u32[]{:S(2)}) %collective-permute-start) | collective-permute-done | bytes 225312 | tf_op jit(solution)/shard_map/while/body/eval_jaxpr/ppermute | solution.py:16
  306.4 10.0 %collective-permute-done = bf16[176,640]{0,1:T(8,128)(2,1)S(1)} collective-permute-done((bf16[176,640]{0,1:T(8,128)(2,1)S(1)}, bf16[176,640]{0,1:T(8,128)(2,1)S(1)}, u32[]{:S(2)}, u32[]{:S(2)}) %collective-permute-start) | collective-permute-done | bytes 225312 | tf_op jit(solution)/shard_map/while/body/eval_jaxpr/ppermute | solution.py:16
  324.3 10.0 %collective-permute-done = bf16[176,640]{0,1:T(8,128)(2,1)S(1)} collective-permute-done((bf16[176,640]{0,1:T(8,128)(2,1)S(1)}, bf16[176,640]{0,1:T(8,128)(2,1)S(1)}, u32[]{:S(2)}, u32[]{:S(2)}) %collective-permute-start) | collective-permute-done | bytes 225312 | tf_op jit(solution)/shard_map/while/body/eval_jaxpr/ppermute | solution.py:16
  342.1 10.0 %collective-permute-done = bf16[176,640]{0,1:T(8,128)(2,1)S(1)} collective-permute-done((bf16[176,640]{0,1:T(8,128)(2,1)S(1)}, bf16[176,640]{0,1:T(8,128)(2,1)S(1)}, u32[]{:S(2)}, u32[]{:S(2)}) %collective-permute-start) | collective-permute-done | bytes 225312 | tf_op jit(solution)/shard_map/while/body/eval_jaxpr/ppermute | solution.py:16
  (332 shorter events, 118.6 us)
Async XLA Ops:
  85.2 2.3 copy-start.2
  90.4 12.0 %collective-permute-start = (bf16[176,640]{0,1:T(8,128)(2,1)S(1)}, bf16[176,640]{0,1:T(8,128)(2,1)S(1)}, u32[]{:S(2)}, u32[]{:S(2)}) collective-permute-start(bf16[176,640]{0,1:T(8,128)(2,1)S(1)} %get-tuple-element.459), channel_id=1, source_target_pairs={{480,0},{0,32},{32,64},{64,96},{96,128},{128,160},{160,192},{192,2... | collective-permute-start | bytes 675848 | tf_op jit(solution)/shard_map/while/body/eval_jaxpr/ppermute | solution.py:16
  103.7 1.1 copy-start.3
  108.3 12.0 %collective-permute-start = (bf16[176,640]{0,1:T(8,128)(2,1)S(1)}, bf16[176,640]{0,1:T(8,128)(2,1)S(1)}, u32[]{:S(2)}, u32[]{:S(2)}) collective-permute-start(bf16[176,640]{0,1:T(8,128)(2,1)S(1)} %get-tuple-element.459), channel_id=1, source_target_pairs={{480,0},{0,32},{32,64},{64,96},{96,128},{128,160},{160,192},{192,2... | collective-permute-start | bytes 675848 | tf_op jit(solution)/shard_map/while/body/eval_jaxpr/ppermute | solution.py:16
  121.5 1.1 copy-start.3
  126.1 12.0 %collective-permute-start = (bf16[176,640]{0,1:T(8,128)(2,1)S(1)}, bf16[176,640]{0,1:T(8,128)(2,1)S(1)}, u32[]{:S(2)}, u32[]{:S(2)}) collective-permute-start(bf16[176,640]{0,1:T(8,128)(2,1)S(1)} %get-tuple-element.459), channel_id=1, source_target_pairs={{480,0},{0,32},{32,64},{64,96},{96,128},{128,160},{160,192},{192,2... | collective-permute-start | bytes 675848 | tf_op jit(solution)/shard_map/while/body/eval_jaxpr/ppermute | solution.py:16
  139.3 1.1 copy-start.3
  143.9 12.0 %collective-permute-start = (bf16[176,640]{0,1:T(8,128)(2,1)S(1)}, bf16[176,640]{0,1:T(8,128)(2,1)S(1)}, u32[]{:S(2)}, u32[]{:S(2)}) collective-permute-start(bf16[176,640]{0,1:T(8,128)(2,1)S(1)} %get-tuple-element.459), channel_id=1, source_target_pairs={{480,0},{0,32},{32,64},{64,96},{96,128},{128,160},{160,192},{192,2... | collective-permute-start | bytes 675848 | tf_op jit(solution)/shard_map/while/body/eval_jaxpr/ppermute | solution.py:16
  157.2 1.1 copy-start.3
  161.8 12.0 %collective-permute-start = (bf16[176,640]{0,1:T(8,128)(2,1)S(1)}, bf16[176,640]{0,1:T(8,128)(2,1)S(1)}, u32[]{:S(2)}, u32[]{:S(2)}) collective-permute-start(bf16[176,640]{0,1:T(8,128)(2,1)S(1)} %get-tuple-element.459), channel_id=1, source_target_pairs={{480,0},{0,32},{32,64},{64,96},{96,128},{128,160},{160,192},{192,2... | collective-permute-start | bytes 675848 | tf_op jit(solution)/shard_map/while/body/eval_jaxpr/ppermute | solution.py:16
  175.0 1.1 copy-start.3
  179.6 12.0 %collective-permute-start = (bf16[176,640]{0,1:T(8,128)(2,1)S(1)}, bf16[176,640]{0,1:T(8,128)(2,1)S(1)}, u32[]{:S(2)}, u32[]{:S(2)}) collective-permute-start(bf16[176,640]{0,1:T(8,128)(2,1)S(1)} %get-tuple-element.459), channel_id=1, source_target_pairs={{480,0},{0,32},{32,64},{64,96},{96,128},{128,160},{160,192},{192,2... | collective-permute-start | bytes 675848 | tf_op jit(solution)/shard_map/while/body/eval_jaxpr/ppermute | solution.py:16
  192.8 1.1 copy-start.3
  197.4 12.0 %collective-permute-start = (bf16[176,640]{0,1:T(8,128)(2,1)S(1)}, bf16[176,640]{0,1:T(8,128)(2,1)S(1)}, u32[]{:S(2)}, u32[]{:S(2)}) collective-permute-start(bf16[176,640]{0,1:T(8,128)(2,1)S(1)} %get-tuple-element.459), channel_id=1, source_target_pairs={{480,0},{0,32},{32,64},{64,96},{96,128},{128,160},{160,192},{192,2... | collective-permute-start | bytes 675848 | tf_op jit(solution)/shard_map/while/body/eval_jaxpr/ppermute | solution.py:16
  210.7 1.1 copy-start.3
  215.3 12.0 %collective-permute-start = (bf16[176,640]{0,1:T(8,128)(2,1)S(1)}, bf16[176,640]{0,1:T(8,128)(2,1)S(1)}, u32[]{:S(2)}, u32[]{:S(2)}) collective-permute-start(bf16[176,640]{0,1:T(8,128)(2,1)S(1)} %get-tuple-element.459), channel_id=1, source_target_pairs={{480,0},{0,32},{32,64},{64,96},{96,128},{128,160},{160,192},{192,2... | collective-permute-start | bytes 675848 | tf_op jit(solution)/shard_map/while/body/eval_jaxpr/ppermute | solution.py:16
  233.1 12.0 %collective-permute-start = (bf16[176,640]{0,1:T(8,128)(2,1)S(1)}, bf16[176,640]{0,1:T(8,128)(2,1)S(1)}, u32[]{:S(2)}, u32[]{:S(2)}) collective-permute-start(bf16[176,640]{0,1:T(8,128)(2,1)S(1)} %get-tuple-element.459), channel_id=1, source_target_pairs={{480,0},{0,32},{32,64},{64,96},{96,128},{128,160},{160,192},{192,2... | collective-permute-start | bytes 675848 | tf_op jit(solution)/shard_map/while/body/eval_jaxpr/ppermute | solution.py:16
  250.9 12.0 %collective-permute-start = (bf16[176,640]{0,1:T(8,128)(2,1)S(1)}, bf16[176,640]{0,1:T(8,128)(2,1)S(1)}, u32[]{:S(2)}, u32[]{:S(2)}) collective-permute-start(bf16[176,640]{0,1:T(8,128)(2,1)S(1)} %get-tuple-element.459), channel_id=1, source_target_pairs={{480,0},{0,32},{32,64},{64,96},{96,128},{128,160},{160,192},{192,2... | collective-permute-start | bytes 675848 | tf_op jit(solution)/shard_map/while/body/eval_jaxpr/ppermute | solution.py:16
  268.8 12.0 %collective-permute-start = (bf16[176,640]{0,1:T(8,128)(2,1)S(1)}, bf16[176,640]{0,1:T(8,128)(2,1)S(1)}, u32[]{:S(2)}, u32[]{:S(2)}) collective-permute-start(bf16[176,640]{0,1:T(8,128)(2,1)S(1)} %get-tuple-element.459), channel_id=1, source_target_pairs={{480,0},{0,32},{32,64},{64,96},{96,128},{128,160},{160,192},{192,2... | collective-permute-start | bytes 675848 | tf_op jit(solution)/shard_map/while/body/eval_jaxpr/ppermute | solution.py:16
  286.6 12.0 %collective-permute-start = (bf16[176,640]{0,1:T(8,128)(2,1)S(1)}, bf16[176,640]{0,1:T(8,128)(2,1)S(1)}, u32[]{:S(2)}, u32[]{:S(2)}) collective-permute-start(bf16[176,640]{0,1:T(8,128)(2,1)S(1)} %get-tuple-element.459), channel_id=1, source_target_pairs={{480,0},{0,32},{32,64},{64,96},{96,128},{128,160},{160,192},{192,2... | collective-permute-start | bytes 675848 | tf_op jit(solution)/shard_map/while/body/eval_jaxpr/ppermute | solution.py:16
  304.4 12.0 %collective-permute-start = (bf16[176,640]{0,1:T(8,128)(2,1)S(1)}, bf16[176,640]{0,1:T(8,128)(2,1)S(1)}, u32[]{:S(2)}, u32[]{:S(2)}) collective-permute-start(bf16[176,640]{0,1:T(8,128)(2,1)S(1)} %get-tuple-element.459), channel_id=1, source_target_pairs={{480,0},{0,32},{32,64},{64,96},{96,128},{128,160},{160,192},{192,2... | collective-permute-start | bytes 675848 | tf_op jit(solution)/shard_map/while/body/eval_jaxpr/ppermute | solution.py:16
  322.3 12.0 %collective-permute-start = (bf16[176,640]{0,1:T(8,128)(2,1)S(1)}, bf16[176,640]{0,1:T(8,128)(2,1)S(1)}, u32[]{:S(2)}, u32[]{:S(2)}) collective-permute-start(bf16[176,640]{0,1:T(8,128)(2,1)S(1)} %get-tuple-element.459), channel_id=1, source_target_pairs={{480,0},{0,32},{32,64},{64,96},{96,128},{128,160},{160,192},{192,2... | collective-permute-start | bytes 675848 | tf_op jit(solution)/shard_map/while/body/eval_jaxpr/ppermute | solution.py:16
  340.1 12.0 %collective-permute-start = (bf16[176,640]{0,1:T(8,128)(2,1)S(1)}, bf16[176,640]{0,1:T(8,128)(2,1)S(1)}, u32[]{:S(2)}, u32[]{:S(2)}) collective-permute-start(bf16[176,640]{0,1:T(8,128)(2,1)S(1)} %get-tuple-element.459), channel_id=1, source_target_pairs={{480,0},{0,32},{32,64},{64,96},{96,128},{128,160},{160,192},{192,2... | collective-permute-start | bytes 675848 | tf_op jit(solution)/shard_map/while/body/eval_jaxpr/ppermute | solution.py:16
  358.0 1.1 copy-start.1
  (10 other events, 10.7 us)
where the time goes:
time: 361 us; the launch traced here: 359 us
  waiting for transfers between devices  151 us (42%)
  blocking collectives  70.2 us (19%)
  other arithmetic  48.3 us (13%)
  matrix products  44.4 us (12%)
  starting transfers between devices  28.8 us (8%)
  local copies, waits for them, and re-layouts  13.3 us (4%)
    ppermute x15, waiting for transfers between devices, shifted(): return lax.ppermute(block, axis, route)  151 us
    all_gather x1, blocking collectives, body(): panel_rows = lax.all_gather(own_seeds, 'wide', axis=0, tiled=True)  70.2 us
    dot_general x16, matrix products, compare(): jnp.einsum('tnw,snw->nts', target_windows, seed_window, preferred_element...  36.8 us
    ppermute x15, starting transfers between devices, shifted(): return lax.ppermute(block, axis, route)  28.8 us
    dynamic_update_slice x15, other arithmetic, record(): lax.dynamic_update_index_in_dim(results[0], dispersion, source, 0)  10.2 us
    div x17, other arithmetic, prepare(): mean_all = jnp.sum(values * weight, axis=1) / total_valid  9.57 us
    reduce_sum x17, other arithmetic, prepare(): spread = jnp.sum(centred * centred, axis=2)  8.51 us
    dot_general x16, matrix products, compare(): jnp.einsum('tf,sf->ts', target_whole, seed_whole, preferred_element_type=...  7.54 us
  transfers between devices with their start and end apart: 15, of which 15 were waited for; matrix products, arithmetic and copies ran while one was open for 0% of the time, Pallas kernels for 0%

commit v1 on v0

--- a/solution.py
+++ b/solution.py
@@ -63,7 +63,8 @@
     total_valid = jnp.sum(scrub_mask.astype(jnp.float32))
     target_windows, target_whole = prepare(series, scrub_mask)
     blocks = lax.axis_size("blk")
-    panel_rows = lax.all_gather(own_seeds, "wide", axis=0, tiled=True)
+    stack = jnp.stack([own_seeds] * lax.axis_size("wide"))
+    panel_rows = jnp.concatenate(lax.all_to_all(stack, "wide", 0, 0), axis=0)
     seed_window, seed_whole = prepare(panel_rows, scrub_mask)
     panel_size = panel_rows.shape[0]
     own_block = lax.axis_index("blk")

time: 361 us -> 323 us (0.89)
  blocking collectives: 70.2 us -> 0 us
  waiting for transfers between devices: 151 us -> 167 us
  starting transfers between devices: 28.8 us -> 44.7 us
  matrix products: 44.4 us -> 54.7 us
  other arithmetic: 48.3 us -> 38.6 us
    all_gather x1 -> x0, blocking collectives: 70.2 us -> none  [body(): panel_rows = lax.all_gather(own_seeds, 'wide', axis=0, tiled=True)]
    all_to_all x0 -> x1, waiting for transfers between devices: none -> 16.3 us  [body(): panel_rows = jnp.concatenate(lax.all_to_all(stack, 'wide', 0, 0), axis=0)]
    all_to_all x0 -> x1, starting transfers between devices: none -> 16.1 us  [body(): panel_rows = jnp.concatenate(lax.all_to_all(stack, 'wide', 0, 0), axis=0)]
    dot_general x16, matrix products: 7.54 us -> 17.7 us  [compare(): jnp.einsum('tf,sf->ts', target_whole, seed_whole, preferred_element_type=...]
    dynamic_update_slice x15, other arithmetic: 10.2 us -> 0.62 us  [record(): lax.dynamic_update_index_in_dim(results[0], dispersion, source, 0)]
  transfers between devices with their start and end apart: 15 -> 16, of which waited for: 15 -> 16; matrix products, arithmetic and copies ran while one was open for 0% -> 2% of each run, Pallas kernels for 0% -> 0%
where the time goes in v1:
time: 323 us; the launch traced here: 322 us
  waiting for transfers between devices  167 us (52%)
  matrix products  54.7 us (17%)
  starting transfers between devices  44.7 us (14%)
  other arithmetic  38.6 us (12%)
  local copies, waits for them, and re-layouts  13.3 us (4%)
    ppermute x15, waiting for transfers between devices, shifted(): return lax.ppermute(block, axis, route)  151 us
    dot_general x16, matrix products, compare(): jnp.einsum('tnw,snw->nts', target_windows, seed_window, preferred_element...  37 us
    ppermute x15, starting transfers between devices, shifted(): return lax.ppermute(block, axis, route)  28.6 us
    dot_general x16, matrix products, compare(): jnp.einsum('tf,sf->ts', target_whole, seed_whole, preferred_element_type=...  17.7 us
    all_to_all x1, waiting for transfers between devices, body(): panel_rows = jnp.concatenate(lax.all_to_all(stack, 'wide', 0, 0), axis=0)  16.3 us
    all_to_all x1, starting transfers between devices, body(): panel_rows = jnp.concatenate(lax.all_to_all(stack, 'wide', 0, 0), axis=0)  16.1 us
    div x17, other arithmetic, prepare(): mean_all = jnp.sum(values * weight, axis=1) / total_valid  9.57 us
    reduce_sum x17, other arithmetic, prepare(): spread = jnp.sum(centred * centred, axis=2)  8.62 us
  transfers between devices with their start and end apart: 16, of which 16 were waited for; matrix products, arithmetic and copies ran while one was open for 2% of the time, Pallas kernels for 0%

profile of v1, /device:TPU:4, one launch (start us, length us, event | category | flops | bytes accessed | tf_op | source)
XLA Modules:
  0.0 321.9 jit_solution(12156885371657415044)
XLA Ops:
  3.7 16.1 %all-to-all-start = ((bf16[32,8,640]{2,1,0:T(8,128)(2,1)}), bf16[32,8,640]{2,1,0:T(8,128)(2,1)S(1)}, u32[]{:S(2)}, u32[]{:S(2)}) async-start(bf16[32,8,640]{2,1,0:T(8,128)(2,1)} %stack.2), calls=%async_computation | async-start | bytes 655360 | tf_op jit(solution)/shard_map/all_to_all | solution.py:67
  28.3 16.3 %all-to-all-done = bf16[32,8,640]{2,1,0:T(8,128)(2,1)S(1)} async-done(((bf16[32,8,640]{2,1,0:T(8,128)(2,1)}), bf16[32,8,640]{2,1,0:T(8,128)(2,1)S(1)}, u32[]{:S(2)}, u32[]{:S(2)}) %all-to-all-start) | async-done | bytes 327712 | tf_op jit(solution)/shard_map/all_to_all | solution.py:67
  49.1 2.3 multiply_reduce_fusion.5
  54.5 266.3 %while.20 = (s32[]{:T(128)}, bf16[16,176,256]{2,1,0:T(8,128)(2,1)S(1)}, bf16[16,176,256]{2,1,0:T(8,128)(2,1)}, bf16[176,640]{0,1:T(8,128)(2,1)S(1)}, f32[20,60]{...) while((s32[]{:T(128)}, ...), condition=%wide.region_20.21_spmd, body=%wide.region_13.20_spmd.sunk | while | flops 177675536 | bytes 21564408 | solution.py:97
  56.5 10.0 %collective-permute-done = bf16[176,640]{0,1:T(8,128)(2,1)S(1)} collective-permute-done((bf16[176,640]{0,1:T(8,128)(2,1)S(1)}, bf16[176,640]{0,1:T(8,128)(2,1)S(1)}, u32[]{:S(2)}, u32[]{:S(2)}) %collective-permute-start) | collective-permute-done | bytes 225312 | tf_op jit(solution)/shard_map/while/body/eval_jaxpr/ppermute | solution.py:16
  74.2 10.0 %collective-permute-done = bf16[176,640]{0,1:T(8,128)(2,1)S(1)} collective-permute-done((bf16[176,640]{0,1:T(8,128)(2,1)S(1)}, bf16[176,640]{0,1:T(8,128)(2,1)S(1)}, u32[]{:S(2)}, u32[]{:S(2)}) %collective-permute-start) | collective-permute-done | bytes 225312 | tf_op jit(solution)/shard_map/while/body/eval_jaxpr/ppermute | solution.py:16
  92.0 10.0 %collective-permute-done = bf16[176,640]{0,1:T(8,128)(2,1)S(1)} collective-permute-done((bf16[176,640]{0,1:T(8,128)(2,1)S(1)}, bf16[176,640]{0,1:T(8,128)(2,1)S(1)}, u32[]{:S(2)}, u32[]{:S(2)}) %collective-permute-start) | collective-permute-done | bytes 225312 | tf_op jit(solution)/shard_map/while/body/eval_jaxpr/ppermute | solution.py:16
  104.3 2.3 multiply_reduce_fusion.19
  109.7 10.0 %collective-permute-done = bf16[176,640]{0,1:T(8,128)(2,1)S(1)} collective-permute-done((bf16[176,640]{0,1:T(8,128)(2,1)S(1)}, bf16[176,640]{0,1:T(8,128)(2,1)S(1)}, u32[]{:S(2)}, u32[]{:S(2)}) %collective-permute-start) | collective-permute-done | bytes 225312 | tf_op jit(solution)/shard_map/while/body/eval_jaxpr/ppermute | solution.py:16
  122.0 2.3 multiply_reduce_fusion.19
  127.5 10.0 %collective-permute-done = bf16[176,640]{0,1:T(8,128)(2,1)S(1)} collective-permute-done((bf16[176,640]{0,1:T(8,128)(2,1)S(1)}, bf16[176,640]{0,1:T(8,128)(2,1)S(1)}, u32[]{:S(2)}, u32[]{:S(2)}) %collective-permute-start) | collective-permute-done | bytes 225312 | tf_op jit(solution)/shard_map/while/body/eval_jaxpr/ppermute | solution.py:16
  139.8 2.3 multiply_reduce_fusion.19
  145.2 10.0 %collective-permute-done = bf16[176,640]{0,1:T(8,128)(2,1)S(1)} collective-permute-done((bf16[176,640]{0,1:T(8,128)(2,1)S(1)}, bf16[176,640]{0,1:T(8,128)(2,1)S(1)}, u32[]{:S(2)}, u32[]{:S(2)}) %collective-permute-start) | collective-permute-done | bytes 225312 | tf_op jit(solution)/shard_map/while/body/eval_jaxpr/ppermute | solution.py:16
  157.5 2.3 multiply_reduce_fusion.19
  163.0 10.0 %collective-permute-done = bf16[176,640]{0,1:T(8,128)(2,1)S(1)} collective-permute-done((bf16[176,640]{0,1:T(8,128)(2,1)S(1)}, bf16[176,640]{0,1:T(8,128)(2,1)S(1)}, u32[]{:S(2)}, u32[]{:S(2)}) %collective-permute-start) | collective-permute-done | bytes 225312 | tf_op jit(solution)/shard_map/while/body/eval_jaxpr/ppermute | solution.py:16
  175.3 2.3 multiply_reduce_fusion.19
  180.8 10.0 %collective-permute-done = bf16[176,640]{0,1:T(8,128)(2,1)S(1)} collective-permute-done((bf16[176,640]{0,1:T(8,128)(2,1)S(1)}, bf16[176,640]{0,1:T(8,128)(2,1)S(1)}, u32[]{:S(2)}, u32[]{:S(2)}) %collective-permute-start) | collective-permute-done | bytes 225312 | tf_op jit(solution)/shard_map/while/body/eval_jaxpr/ppermute | solution.py:16
  198.5 10.0 %collective-permute-done = bf16[176,640]{0,1:T(8,128)(2,1)S(1)} collective-permute-done((bf16[176,640]{0,1:T(8,128)(2,1)S(1)}, bf16[176,640]{0,1:T(8,128)(2,1)S(1)}, u32[]{:S(2)}, u32[]{:S(2)}) %collective-permute-start) | collective-permute-done | bytes 225312 | tf_op jit(solution)/shard_map/while/body/eval_jaxpr/ppermute | solution.py:16
  216.3 10.0 %collective-permute-done = bf16[176,640]{0,1:T(8,128)(2,1)S(1)} collective-permute-done((bf16[176,640]{0,1:T(8,128)(2,1)S(1)}, bf16[176,640]{0,1:T(8,128)(2,1)S(1)}, u32[]{:S(2)}, u32[]{:S(2)}) %collective-permute-start) | collective-permute-done | bytes 225312 | tf_op jit(solution)/shard_map/while/body/eval_jaxpr/ppermute | solution.py:16
  234.0 10.0 %collective-permute-done = bf16[176,640]{0,1:T(8,128)(2,1)S(1)} collective-permute-done((bf16[176,640]{0,1:T(8,128)(2,1)S(1)}, bf16[176,640]{0,1:T(8,128)(2,1)S(1)}, u32[]{:S(2)}, u32[]{:S(2)}) %collective-permute-start) | collective-permute-done | bytes 225312 | tf_op jit(solution)/shard_map/while/body/eval_jaxpr/ppermute | solution.py:16
  251.8 10.0 %collective-permute-done = bf16[176,640]{0,1:T(8,128)(2,1)S(1)} collective-permute-done((bf16[176,640]{0,1:T(8,128)(2,1)S(1)}, bf16[176,640]{0,1:T(8,128)(2,1)S(1)}, u32[]{:S(2)}, u32[]{:S(2)}) %collective-permute-start) | collective-permute-done | bytes 225312 | tf_op jit(solution)/shard_map/while/body/eval_jaxpr/ppermute | solution.py:16
  269.5 10.0 %collective-permute-done = bf16[176,640]{0,1:T(8,128)(2,1)S(1)} collective-permute-done((bf16[176,640]{0,1:T(8,128)(2,1)S(1)}, bf16[176,640]{0,1:T(8,128)(2,1)S(1)}, u32[]{:S(2)}, u32[]{:S(2)}) %collective-permute-start) | collective-permute-done | bytes 225312 | tf_op jit(solution)/shard_map/while/body/eval_jaxpr/ppermute | solution.py:16
  287.3 10.0 %collective-permute-done = bf16[176,640]{0,1:T(8,128)(2,1)S(1)} collective-permute-done((bf16[176,640]{0,1:T(8,128)(2,1)S(1)}, bf16[176,640]{0,1:T(8,128)(2,1)S(1)}, u32[]{:S(2)}, u32[]{:S(2)}) %collective-permute-start) | collective-permute-done | bytes 225312 | tf_op jit(solution)/shard_map/while/body/eval_jaxpr/ppermute | solution.py:16
  305.0 10.0 %collective-permute-done = bf16[176,640]{0,1:T(8,128)(2,1)S(1)} collective-permute-done((bf16[176,640]{0,1:T(8,128)(2,1)S(1)}, bf16[176,640]{0,1:T(8,128)(2,1)S(1)}, u32[]{:S(2)}, u32[]{:S(2)}) %collective-permute-start) | collective-permute-done | bytes 225312 | tf_op jit(solution)/shard_map/while/body/eval_jaxpr/ppermute | solution.py:16
  (382 shorter events, 121.3 us)
Async XLA Ops:
  0.6 22.9 %copy-start = (bf16[176,640]{1,0:T(8,128)(2,1)S(1)}, bf16[176,640]{1,0:T(8,128)(2,1)}, u32[]{:S(2)}) copy-start(bf16[176,640]{1,0:T(8,128)(2,1)} %param.5) | copy-start | bytes 675844
  3.7 40.9 %all-to-all-start = ((bf16[32,8,640]{2,1,0:T(8,128)(2,1)}), bf16[32,8,640]{2,1,0:T(8,128)(2,1)S(1)}, u32[]{:S(2)}, u32[]{:S(2)}) async-start(bf16[32,8,640]{2,1,0:T(8,128)(2,1)} %stack.2), calls=%async_computation | async-start | bytes 655360 | tf_op jit(solution)/shard_map/all_to_all | solution.py:67
  26.0 21.8 %copy-start.6 = (f32[20]{0:T(128)}, f32[20]{0:T(128)S(1)}, u32[]{:S(2)}) copy-start(f32[20]{0:T(128)S(1)} %reduce_sum.264) | copy-start | bytes 244
  26.6 18.0 %copy-start.4 = (f32[176,20]{0,1:T(8,128)}, f32[176,20]{0,1:T(8,128)S(1)}, u32[]{:S(2)}) copy-start(f32[176,20]{0,1:T(8,128)S(1)} %broadcast_divide_fusion.3) | copy-start | bytes 42244
  54.5 12.9 %copy-start.1 = (bf16[16,176,256]{2,1,0:T(8,128)(2,1)}, bf16[16,176,256]{2,1,0:T(8,128)(2,1)S(1)}, u32[]{:S(2)}) copy-start(bf16[16,176,256]{2,1,0:T(8,128)(2,1)S(1)} %get-tuple-element.457) | copy-start | bytes 4325380 | tf_op jit(solution)/shard_map/while
  54.5 12.0 %collective-permute-start = (bf16[176,640]{0,1:T(8,128)(2,1)S(1)}, bf16[176,640]{0,1:T(8,128)(2,1)S(1)}, u32[]{:S(2)}, u32[]{:S(2)}) collective-permute-start(bf16[176,640]{0,1:T(8,128)(2,1)S(1)} %get-tuple-element.459), channel_id=1, source_target_pairs={{480,0},{0,32},{32,64},{64,96},{96,128},{128,160},{160,192},{192,2... | collective-permute-start | bytes 675848 | tf_op jit(solution)/shard_map/while/body/eval_jaxpr/ppermute | solution.py:16
  72.3 12.0 %collective-permute-start = (bf16[176,640]{0,1:T(8,128)(2,1)S(1)}, bf16[176,640]{0,1:T(8,128)(2,1)S(1)}, u32[]{:S(2)}, u32[]{:S(2)}) collective-permute-start(bf16[176,640]{0,1:T(8,128)(2,1)S(1)} %get-tuple-element.459), channel_id=1, source_target_pairs={{480,0},{0,32},{32,64},{64,96},{96,128},{128,160},{160,192},{192,2... | collective-permute-start | bytes 675848 | tf_op jit(solution)/shard_map/while/body/eval_jaxpr/ppermute | solution.py:16
  90.0 12.0 %collective-permute-start = (bf16[176,640]{0,1:T(8,128)(2,1)S(1)}, bf16[176,640]{0,1:T(8,128)(2,1)S(1)}, u32[]{:S(2)}, u32[]{:S(2)}) collective-permute-start(bf16[176,640]{0,1:T(8,128)(2,1)S(1)} %get-tuple-element.459), channel_id=1, source_target_pairs={{480,0},{0,32},{32,64},{64,96},{96,128},{128,160},{160,192},{192,2... | collective-permute-start | bytes 675848 | tf_op jit(solution)/shard_map/while/body/eval_jaxpr/ppermute | solution.py:16
  107.8 12.0 %collective-permute-start = (bf16[176,640]{0,1:T(8,128)(2,1)S(1)}, bf16[176,640]{0,1:T(8,128)(2,1)S(1)}, u32[]{:S(2)}, u32[]{:S(2)}) collective-permute-start(bf16[176,640]{0,1:T(8,128)(2,1)S(1)} %get-tuple-element.459), channel_id=1, source_target_pairs={{480,0},{0,32},{32,64},{64,96},{96,128},{128,160},{160,192},{192,2... | collective-permute-start | bytes 675848 | tf_op jit(solution)/shard_map/while/body/eval_jaxpr/ppermute | solution.py:16
  125.5 12.0 %collective-permute-start = (bf16[176,640]{0,1:T(8,128)(2,1)S(1)}, bf16[176,640]{0,1:T(8,128)(2,1)S(1)}, u32[]{:S(2)}, u32[]{:S(2)}) collective-permute-start(bf16[176,640]{0,1:T(8,128)(2,1)S(1)} %get-tuple-element.459), channel_id=1, source_target_pairs={{480,0},{0,32},{32,64},{64,96},{96,128},{128,160},{160,192},{192,2... | collective-permute-start | bytes 675848 | tf_op jit(solution)/shard_map/while/body/eval_jaxpr/ppermute | solution.py:16
  143.3 12.0 %collective-permute-start = (bf16[176,640]{0,1:T(8,128)(2,1)S(1)}, bf16[176,640]{0,1:T(8,128)(2,1)S(1)}, u32[]{:S(2)}, u32[]{:S(2)}) collective-permute-start(bf16[176,640]{0,1:T(8,128)(2,1)S(1)} %get-tuple-element.459), channel_id=1, source_target_pairs={{480,0},{0,32},{32,64},{64,96},{96,128},{128,160},{160,192},{192,2... | collective-permute-start | bytes 675848 | tf_op jit(solution)/shard_map/while/body/eval_jaxpr/ppermute | solution.py:16
  161.0 12.0 %collective-permute-start = (bf16[176,640]{0,1:T(8,128)(2,1)S(1)}, bf16[176,640]{0,1:T(8,128)(2,1)S(1)}, u32[]{:S(2)}, u32[]{:S(2)}) collective-permute-start(bf16[176,640]{0,1:T(8,128)(2,1)S(1)} %get-tuple-element.459), channel_id=1, source_target_pairs={{480,0},{0,32},{32,64},{64,96},{96,128},{128,160},{160,192},{192,2... | collective-permute-start | bytes 675848 | tf_op jit(solution)/shard_map/while/body/eval_jaxpr/ppermute | solution.py:16
  178.8 12.0 %collective-permute-start = (bf16[176,640]{0,1:T(8,128)(2,1)S(1)}, bf16[176,640]{0,1:T(8,128)(2,1)S(1)}, u32[]{:S(2)}, u32[]{:S(2)}) collective-permute-start(bf16[176,640]{0,1:T(8,128)(2,1)S(1)} %get-tuple-element.459), channel_id=1, source_target_pairs={{480,0},{0,32},{32,64},{64,96},{96,128},{128,160},{160,192},{192,2... | collective-permute-start | bytes 675848 | tf_op jit(solution)/shard_map/while/body/eval_jaxpr/ppermute | solution.py:16
  196.5 12.0 %collective-permute-start = (bf16[176,640]{0,1:T(8,128)(2,1)S(1)}, bf16[176,640]{0,1:T(8,128)(2,1)S(1)}, u32[]{:S(2)}, u32[]{:S(2)}) collective-permute-start(bf16[176,640]{0,1:T(8,128)(2,1)S(1)} %get-tuple-element.459), channel_id=1, source_target_pairs={{480,0},{0,32},{32,64},{64,96},{96,128},{128,160},{160,192},{192,2... | collective-permute-start | bytes 675848 | tf_op jit(solution)/shard_map/while/body/eval_jaxpr/ppermute | solution.py:16
  214.3 12.0 %collective-permute-start = (bf16[176,640]{0,1:T(8,128)(2,1)S(1)}, bf16[176,640]{0,1:T(8,128)(2,1)S(1)}, u32[]{:S(2)}, u32[]{:S(2)}) collective-permute-start(bf16[176,640]{0,1:T(8,128)(2,1)S(1)} %get-tuple-element.459), channel_id=1, source_target_pairs={{480,0},{0,32},{32,64},{64,96},{96,128},{128,160},{160,192},{192,2... | collective-permute-start | bytes 675848 | tf_op jit(solution)/shard_map/while/body/eval_jaxpr/ppermute | solution.py:16
  232.0 12.9 %copy-start.1 = (bf16[16,176,256]{2,1,0:T(8,128)(2,1)}, bf16[16,176,256]{2,1,0:T(8,128)(2,1)S(1)}, u32[]{:S(2)}) copy-start(bf16[16,176,256]{2,1,0:T(8,128)(2,1)S(1)} %get-tuple-element.457) | copy-start | bytes 4325380 | tf_op jit(solution)/shard_map/while
  232.0 12.0 %collective-permute-start = (bf16[176,640]{0,1:T(8,128)(2,1)S(1)}, bf16[176,640]{0,1:T(8,128)(2,1)S(1)}, u32[]{:S(2)}, u32[]{:S(2)}) collective-permute-start(bf16[176,640]{0,1:T(8,128)(2,1)S(1)} %get-tuple-element.459), channel_id=1, source_target_pairs={{480,0},{0,32},{32,64},{64,96},{96,128},{128,160},{160,192},{192,2... | collective-permute-start | bytes 675848 | tf_op jit(solution)/shard_map/while/body/eval_jaxpr/ppermute | solution.py:16
  249.8 12.9 %copy-start.1 = (bf16[16,176,256]{2,1,0:T(8,128)(2,1)}, bf16[16,176,256]{2,1,0:T(8,128)(2,1)S(1)}, u32[]{:S(2)}) copy-start(bf16[16,176,256]{2,1,0:T(8,128)(2,1)S(1)} %get-tuple-element.457) | copy-start | bytes 4325380 | tf_op jit(solution)/shard_map/while
  249.8 12.0 %collective-permute-start = (bf16[176,640]{0,1:T(8,128)(2,1)S(1)}, bf16[176,640]{0,1:T(8,128)(2,1)S(1)}, u32[]{:S(2)}, u32[]{:S(2)}) collective-permute-start(bf16[176,640]{0,1:T(8,128)(2,1)S(1)} %get-tuple-element.459), channel_id=1, source_target_pairs={{480,0},{0,32},{32,64},{64,96},{96,128},{128,160},{160,192},{192,2... | collective-permute-start | bytes 675848 | tf_op jit(solution)/shard_map/while/body/eval_jaxpr/ppermute | solution.py:16
  267.5 12.9 %copy-start.1 = (bf16[16,176,256]{2,1,0:T(8,128)(2,1)}, bf16[16,176,256]{2,1,0:T(8,128)(2,1)S(1)}, u32[]{:S(2)}) copy-start(bf16[16,176,256]{2,1,0:T(8,128)(2,1)S(1)} %get-tuple-element.457) | copy-start | bytes 4325380 | tf_op jit(solution)/shard_map/while
  267.5 12.0 %collective-permute-start = (bf16[176,640]{0,1:T(8,128)(2,1)S(1)}, bf16[176,640]{0,1:T(8,128)(2,1)S(1)}, u32[]{:S(2)}, u32[]{:S(2)}) collective-permute-start(bf16[176,640]{0,1:T(8,128)(2,1)S(1)} %get-tuple-element.459), channel_id=1, source_target_pairs={{480,0},{0,32},{32,64},{64,96},{96,128},{128,160},{160,192},{192,2... | collective-permute-start | bytes 675848 | tf_op jit(solution)/shard_map/while/body/eval_jaxpr/ppermute | solution.py:16
  285.3 12.9 %copy-start.1 = (bf16[16,176,256]{2,1,0:T(8,128)(2,1)}, bf16[16,176,256]{2,1,0:T(8,128)(2,1)S(1)}, u32[]{:S(2)}) copy-start(bf16[16,176,256]{2,1,0:T(8,128)(2,1)S(1)} %get-tuple-element.457) | copy-start | bytes 4325380 | tf_op jit(solution)/shard_map/while
  285.3 12.0 %collective-permute-start = (bf16[176,640]{0,1:T(8,128)(2,1)S(1)}, bf16[176,640]{0,1:T(8,128)(2,1)S(1)}, u32[]{:S(2)}, u32[]{:S(2)}) collective-permute-start(bf16[176,640]{0,1:T(8,128)(2,1)S(1)} %get-tuple-element.459), channel_id=1, source_target_pairs={{480,0},{0,32},{32,64},{64,96},{96,128},{128,160},{160,192},{192,2... | collective-permute-start | bytes 675848 | tf_op jit(solution)/shard_map/while/body/eval_jaxpr/ppermute | solution.py:16
  303.1 12.0 %collective-permute-start = (bf16[176,640]{0,1:T(8,128)(2,1)S(1)}, bf16[176,640]{0,1:T(8,128)(2,1)S(1)}, u32[]{:S(2)}, u32[]{:S(2)}) collective-permute-start(bf16[176,640]{0,1:T(8,128)(2,1)S(1)} %get-tuple-element.459), channel_id=1, source_target_pairs={{480,0},{0,32},{32,64},{64,96},{96,128},{128,160},{160,192},{192,2... | collective-permute-start | bytes 675848 | tf_op jit(solution)/shard_map/while/body/eval_jaxpr/ppermute | solution.py:16
  (34 other events, 174.7 us)
